TPU v7x, 256 devices: a whole 4x4x8 slice. The times are simulated.
256 devices in a mesh: row: 32 (over z, x_lo, core), feat: 8 (over y, x_hi).
Axes of the slice: x: 4 (x_hi: 2, x_lo: 2; x = x_hi * 2 + x_lo), y: 4, z: 8, core: 2. Of those that a mesh axis runs over, the one named last changes fastest.
Arguments:
- vectors: bfloat16 [81920, 1024], P('row', 'feat')
- rotation: bfloat16 [1024, 1024], P('feat')
- codes: int32 [81920, 64], P('row', 'feat'), may hold values from 0 to 255
- live_rows: int32 [32], P('row'), may hold values from 640 to 2560
Outputs:
- centroids: float32 [256, 1024], P('row', 'feat')
- grad_t: float32 [1024, 1024], P('row', 'feat')
All inputs are finite; a program needn't handle non-finite values.
Results may differ from a plain program's by a relative error of at most 0.00094.
Values may be sent and summed in bfloat16 or wider, within the bound.
No kernel may reach another device: no remote copies, remote signals or barrier semaphores. Data moves between devices by JAX's collectives and lax.ppermute only.
A program may use at most 64 MiB of HBM per device.

v0:
```python
import math
import jax
import jax.numpy as jnp
from jax import lax
from jax.sharding import PartitionSpec as P

K = 256


def make_hot(code_block, keeper):
    kinds = jnp.arange(K, dtype=jnp.int32)
    return (code_block[:, :, None] == kinds[None, None, :]).astype(jnp.bfloat16) * keeper[
        :, None, None
    ]


def rebuild(hot, table_part, groups, depth):
    rows = hot.shape[0]
    shaped = table_part.reshape(K, groups, depth)
    joined = jnp.einsum("nmk,kmd->nmd", hot, shaped, preferred_element_type=jnp.float32)
    return joined.reshape(rows, groups * depth).astype(jnp.bfloat16)


def blocked_sums(hot, rotated, groups, depth):
    rows = hot.shape[0]
    step_rows = math.gcd(rows, 512)
    turns = rows // step_rows

    def add_block(index, total):
        hot_block = lax.dynamic_slice_in_dim(hot, index * step_rows, step_rows, 0).astype(
            jnp.float32
        )
        rot_block = lax.dynamic_slice_in_dim(rotated, index * step_rows, step_rows, 0).reshape(
            step_rows, groups, depth
        )
        return total + jnp.einsum(
            "nmk,nmd->kmd", hot_block, rot_block, precision=lax.Precision.HIGHEST
        )

    start = jnp.zeros((K, groups, depth), jnp.float32)
    return lax.fori_loop(0, turns, add_block, start).reshape(K, groups * depth)


def shards(vectors, rotation, codes, live_rows):
    rows = vectors.shape[0]
    local = vectors.shape[1]
    groups = codes.shape[1]
    depth = local // groups
    keeper = (jnp.arange(rows, dtype=jnp.int32) < live_rows[0]).astype(jnp.bfloat16)
    hot = make_hot(codes, keeper)
    counts = jnp.sum(hot, axis=0, dtype=jnp.float32).T
    partial_value = jnp.dot(vectors, rotation, preferred_element_type=jnp.float32)
    rotated = lax.psum_scatter(partial_value, "feat", scatter_dimension=1, tiled=True)
    sums = blocked_sums(hot, rotated, groups, depth)
    share_sums, share_counts = (
        lax.psum_scatter(sums, "row", scatter_dimension=0, tiled=True),
        lax.psum_scatter(counts, "row", scatter_dimension=0, tiled=True),
    )
    centroids = share_sums / (jnp.repeat(share_counts, depth, axis=1) + 1.0)
    table = lax.all_gather(centroids.astype(jnp.bfloat16), "row", axis=0, tiled=True)
    local_recon = rebuild(hot, table, groups, depth)
    recon = lax.all_gather(local_recon, "feat", axis=1, tiled=True)
    inverse = 1.0 / (rows * lax.axis_size("row"))
    product = lax.dot_general(
        recon, vectors, (((0,), (0,)), ((), ())), preferred_element_type=jnp.float32
    )
    grad_t = lax.psum_scatter(product * inverse, "row", scatter_dimension=0, tiled=True)
    return (centroids, grad_t)


def solution(mesh):
    return jax.shard_map(
        shards,
        mesh=mesh,
        in_specs=(P("row", "feat"), P("feat", None), P("row", "feat"), P("row")),
        out_specs=(P("row", "feat"), P("row", "feat")),
        check_vma=False,
    )
```

profile of v0, /device:TPU:4, one launch (start us, length us, event | category | flops | bytes accessed | tf_op | source)
XLA Modules:
  0.0 625.4 jit_solution(6406891080240727840)
XLA Ops:
  7.2 0.0 copy-start
  7.2 0.0 copy-start.2
  7.2 0.0 reduce-scatter.5.cloned.1.call-start
  7.2 1.0 copy-done
  8.3 6.4 %fusion.20 = f32[2560,1024]{1,0:T(8,128)} fusion(bf16[2560,128]{1,0:T(8,128)(2,1)S(1)} %copy-done, bf16[128,1024]{1,0:T(8,128)(2,1)} %param.7), kind=kOutput, calls=%fused_computation.20 | convolution fusion | flops 671088640 | bytes 11403264 | tf_op jit(solution)/shard_map/dot_general | solution.py:52
  14.7 0.0 reduce-scatter.5.cloned.1.call-update
  14.7 0.0 all-reduce.4.cloned.1.call-start
  15.4 0.0 copy-done.2
  15.4 5.4 fusion.9
  20.9 0.0 copy-start.3
  20.9 133.1 %reduce-scatter.5.cloned.1.call-done = f32[2560,128]{1,0:T(8,128)} async-done(((f32[2560,1024]{1,0:T(8,128)}), f32[2560,128]{1,0:T(8,128)}) %reduce-scatter.5.cloned.1.call-update) | async-done | bytes 1310736 | tf_op jit(solution)/shard_map/reduce_scatter | solution.py:53
  153.9 18.3 %while.14 = (s32[]{:T(128)}, f32[256,8,16]{0,2,1:T(8,128)S(1)}, f32[2560,128]{1,0:T(8,128)}, bf16[2560,8,256]{2,0,1:T(8,128)(2,1)}, s32[]{:T(128)}, /*index=5*/s32[]{:T(128)}, s32[]{:T(128)}, s32[]{:T(128)}) while((s32[]{:T(128)}, f32[256,8,16]{0,2,1:T(8,128)S(1)}, f32[2560,128]{1,0:T(8,128)}, bf16[2560,8,256]{2,0,1:T(8,128)(2,1)}, ...), condition=%wide.region_2.0_spmd.clone, body=%wide.region_1.0_spmd.clone.sunk | while | flops 201392128 | bytes 3670173 | solution.py:41
  153.9 1.0 constant_dynamic-slice_fusion.2
  154.9 0.1 copy.21
  155.1 2.5 fusion.32
  157.6 1.0 constant_dynamic-slice_fusion.2
  158.6 0.1 copy.21
  158.7 2.5 fusion.32
  161.3 1.0 constant_dynamic-slice_fusion.2
  162.3 0.1 copy.21
  162.4 2.5 fusion.32
  164.9 1.0 constant_dynamic-slice_fusion.2
  165.9 0.1 copy.21
  166.1 2.5 fusion.32
  168.6 1.0 constant_dynamic-slice_fusion.2
  169.6 0.1 copy.21
  169.7 2.5 fusion.32
  172.3 0.6 copy-done.1
  172.9 0.0 all-reduce.4.cloned.1.call-update
  172.9 0.0 all-gather.2.cloned.1.call-start
  173.0 4.6 convert_reduce_fusion
  177.6 0.0 copy-done.3
  177.6 0.6 dynamic-slice
  178.9 57.8 %all-reduce.1 = f32[256,8]{0,1:T(8,128)S(1)} all-reduce(f32[256,8]{0,1:T(8,128)S(1)} %bitcast.37), channel_id=4, replica_groups=mesh['row'=32,'feat'=8] {'row'}, use_global_device_ids=true, to_apply=%region_5.0.clone | all-reduce | flops 2048 | bytes 16384
  236.7 0.1 dynamic-slice_add_fusion
  236.8 138.9 %all-reduce.4.cloned.1.call-done = f32[256,128]{0,1:T(8,128)} async-done(((f32[256,128]{0,1:T(8,128)}), f32[256,128]{0,1:T(8,128)}) %all-reduce.4.cloned.1.call-update) | async-done | bytes 131088
  375.6 0.9 fusion.19
  376.5 0.1 copy.12
  376.6 30.6 %all_gather.6 = bf16[256,128]{1,0:T(8,128)(2,1)S(1)} all-gather(bf16[8,128]{1,0:T(8,128)(2,1)S(1)} %copy.12), channel_id=1, replica_groups=mesh['row'=32,'feat'=8] {'row'}, dimensions={0}, use_global_device_ids=true | all-gather | bytes 67584 | tf_op jit(solution)/shard_map/all_gather | solution.py:60
  407.2 0.1 copy.13
  407.3 6.3 %fusion.14 = bf16[8,16,2560]{2,1,0:T(8,128)(2,1)} fusion(bf16[256,8,16]{0,2,1:T(8,128)(2,1)S(1)} %bitcast.36, s32[2560,8]{0,1:T(8,128)S(1)} %copy-done.2, bf16[2560]{0:T(1024)(128)(2,1)S(1)} %fusion.17), kind=kOutput, calls=%fused_computation.12 | convolution fusion | flops 178585600 | bytes 807936 | tf_op jit(solution)/shard_map/nmk,kmd->nmd/dot_general | solution.py:20
  413.6 0.0 all-gather.2.cloned.1.call-update
  413.6 0.0 reduce-scatter.7.cloned.1.call-start
  413.7 84.3 %all-gather.2.cloned.1.call-done = bf16[2560,1024]{0,1:T(8,128)(2,1)} async-done(((bf16[2560,128]{0,1:T(8,128)(2,1)}), bf16[2560,1024]{0,1:T(8,128)(2,1)}) %all-gather.2.cloned.1.call-update) | async-done | bytes 5242896 | tf_op jit(solution)/shard_map/all_gather | solution.py:62
  497.9 4.8 convolution_multiply_fusion
  502.8 0.0 reduce-scatter.7.cloned.1.call-update
  502.8 0.7 copy.14
  503.4 115.5 %reduce-scatter.7.cloned.1.call-done = f32[32,128]{1,0:T(8,128)} async-done(((f32[1024,128]{1,0:T(8,128)}), f32[32,128]{1,0:T(8,128)}) %reduce-scatter.7.cloned.1.call-update) | async-done | bytes 16400 | tf_op jit(solution)/shard_map/reduce_scatter | solution.py:67
  (3 shorter events, 0.0 us)
Async XLA Ops:
  7.2 1.1 copy-start
  7.2 8.3 %copy-start.2 = (s32[2560,8]{0,1:T(8,128)S(1)}, s32[2560,8]{0,1:T(8,128)}, u32[]{:S(2)}) copy-start(s32[2560,8]{0,1:T(8,128)} %param.8) | copy-start | bytes 245764
  7.2 146.8 %reduce-scatter.5.cloned.1.call-start = ((), (), s32[]{:S(2)}) async-start(), calls=%async_computation.2 | async-start | bytes 11796480 | tf_op jit(solution)/shard_map/reduce_scatter | solution.py:53
  14.7 360.9 %all-reduce.4.cloned.1.call-start = ((), (), s32[]{:S(2)}) async-start(), calls=%async_computation.5 | async-start | bytes 262144
  20.9 156.7 %copy-start.3 = (u32[256]{0:T(256)S(1)}, u32[256]{0:T(256)}, u32[]{:S(2)}) copy-start(u32[256]{0:T(256)} %constant.42) | copy-start | bytes 3076
  172.3 0.6 copy-start.1
  172.9 325.0 %all-gather.2.cloned.1.call-start = ((), (), s32[]{:S(2)}) async-start(), calls=%async_computation.3 | async-start | bytes 5898240 | tf_op jit(solution)/shard_map/all_gather | solution.py:62
  413.6 205.3 %reduce-scatter.7.cloned.1.call-start = ((), (), s32[]{:S(2)}) async-start(), calls=%async_computation.4 | async-start | bytes 540672 | tf_op jit(solution)/shard_map/reduce_scatter | solution.py:67
Sparse Core Ops, SparseCore 0:
  14.8 139.0 reduce-scatter.4
  173.1 202.5 all-reduce.3
  413.7 84.1 all-gather.1
  502.9 115.9 reduce-scatter.6
where the time goes:
time: 626 us; the launch traced here: 625 us
  waiting for transfers between devices  472 us (75%)
  blocking collectives  88.4 us (14%)
  matrix products  30.3 us (5%)
  between operations  15.1 us (2%)
  other arithmetic  11.1 us (2%)
  local copies, waits for them, and re-layouts  8.63 us (1%)
    unnamed x5, waiting for transfers between devices  139 us
    reduce_scatter x1, waiting for transfers between devices, shards(): lax.psum_scatter(partial_value, 'feat', scatter_dimension=1, tiled=True)  133 us
    reduce_scatter x1, waiting for transfers between devices, shards(): lax.psum_scatter(product * inverse, 'row', scatter_dimension=0, tiled=True)  115 us
    all_gather x1, waiting for transfers between devices, shards(): recon = lax.all_gather(local_recon, 'feat', axis=1, tiled=True)  84.3 us
    unnamed x1, blocking collectives  57.8 us
    all_gather x1, blocking collectives, shards(): lax.all_gather(centroids.astype(jnp.bfloat16), 'row', axis=0, tiled=True)  30.6 us
    dot_general x5, matrix products, add_block(): jnp.einsum('nmk,nmd->kmd', hot_block, rot_block, precision=lax.Precision....  12.7 us
  transfers between devices with their start and end apart: 4, of which 4 were waited for; matrix products, arithmetic and copies ran while one was open for 2% of the time, Pallas kernels for 0%

commit v1 on v0

--- a/solution.py
+++ b/solution.py
@@ -3,6 +3,7 @@
 import jax.numpy as jnp
 from jax import lax
 from jax.sharding import PartitionSpec as P
+from jax.lax import all_to_all, axis_size
 
 K = 256
 
@@ -42,6 +43,12 @@
 
 
 def shards(vectors, rotation, codes, live_rows):
+
+    def bring_steps_all(t0, array_axis):
+        return jnp.concatenate(
+            all_to_all(jnp.stack([t0 for _ in range(axis_size("feat"))]), "feat", 0, 0), array_axis
+        )
+
     rows = vectors.shape[0]
     local = vectors.shape[1]
     groups = codes.shape[1]
@@ -59,7 +66,7 @@
     centroids = share_sums / (jnp.repeat(share_counts, depth, axis=1) + 1.0)
     table = lax.all_gather(centroids.astype(jnp.bfloat16), "row", axis=0, tiled=True)
     local_recon = rebuild(hot, table, groups, depth)
-    recon = lax.all_gather(local_recon, "feat", axis=1, tiled=True)
+    recon = bring_steps_all(local_recon, 1)
     inverse = 1.0 / (rows * lax.axis_size("row"))
     product = lax.dot_general(
         recon, vectors, (((0,), (0,)), ((), ())), preferred_element_type=jnp.float32

time: 626 us -> 607 us (0.970)
  waiting for transfers between devices: 472 us -> 386 us
  blocking collectives: 88.4 us -> 155 us
    all_gather x1 -> x0, waiting for transfers between devices: 84.3 us -> none  [shards(): recon = lax.all_gather(local_recon, 'feat', axis=1, tiled=True)]
    all_to_all x0 -> x1, blocking collectives: none -> 67 us  [bring_steps_all(): all_to_all(jnp.stack([t0 for _ in range(axis_size('feat'))]), 'feat', 0, 0)]
    unnamed x5 -> x4, waiting for transfers between devices: 139 us -> 139 us
  transfers between devices with their start and end apart: 4 -> 3, of which waited for: 4 -> 3; matrix products, arithmetic and copies ran while one was open for 2% -> 2% of each run, Pallas kernels for 0% -> 0%
where the time goes in v1:
time: 607 us; the launch traced here: 606 us
  waiting for transfers between devices  386 us (64%)
  blocking collectives  155 us (26%)
  matrix products  28.6 us (5%)
  between operations  15.1 us (2%)
  other arithmetic  11.1 us (2%)
  local copies, waits for them, and re-layouts  9.08 us (1%)
    unnamed x4, waiting for transfers between devices  139 us
    reduce_scatter x1, waiting for transfers between devices, shards(): lax.psum_scatter(partial_value, 'feat', scatter_dimension=1, tiled=True)  133 us
    reduce_scatter x1, waiting for transfers between devices, shards(): lax.psum_scatter(product * inverse, 'row', scatter_dimension=0, tiled=True)  114 us
    all_to_all x1, blocking collectives, bring_steps_all(): all_to_all(jnp.stack([t0 for _ in range(axis_size('feat'))]), 'feat', 0, 0)  67 us
    unnamed x1, blocking collectives  57.8 us
    all_gather x1, blocking collectives, shards(): lax.all_gather(centroids.astype(jnp.bfloat16), 'row', axis=0, tiled=True)  30.6 us
    dot_general x5, matrix products, add_block(): jnp.einsum('nmk,nmd->kmd', hot_block, rot_block, precision=lax.Precision....  12.7 us
  transfers between devices with their start and end apart: 3, of which 3 were waited for; matrix products, arithmetic and copies ran while one was open for 2% of the time, Pallas kernels for 0%

profile of v1, /device:TPU:4, one launch (start us, length us, event | category | flops | bytes accessed | tf_op | source)
XLA Modules:
  0.0 605.7 jit_solution(12096597548809295441)
XLA Ops:
  7.2 0.0 copy-start
  7.2 0.0 copy-start.2
  7.2 0.0 reduce-scatter.5.cloned.1.call-start
  7.2 1.0 copy-done
  8.3 6.4 %fusion.20 = f32[2560,1024]{1,0:T(8,128)} fusion(bf16[2560,128]{1,0:T(8,128)(2,1)S(1)} %copy-done, bf16[128,1024]{1,0:T(8,128)(2,1)} %param.7), kind=kOutput, calls=%fused_computation.20 | convolution fusion | flops 671088640 | bytes 11403264 | tf_op jit(solution)/shard_map/dot_general | solution.py:59
  14.7 0.0 reduce-scatter.5.cloned.1.call-update
  14.7 0.0 all-reduce.4.cloned.1.call-start
  15.4 0.0 copy-done.2
  15.5 5.5 fusion.9
  20.9 0.0 copy-start.3
  20.9 133.0 %reduce-scatter.5.cloned.1.call-done = f32[2560,128]{1,0:T(8,128)} async-done(((f32[2560,1024]{1,0:T(8,128)}), f32[2560,128]{1,0:T(8,128)}) %reduce-scatter.5.cloned.1.call-update) | async-done | bytes 1310736 | tf_op jit(solution)/shard_map/reduce_scatter | solution.py:60
  154.0 18.3 %while.14 = (s32[]{:T(128)}, f32[256,8,16]{0,2,1:T(8,128)S(1)}, f32[2560,128]{1,0:T(8,128)}, bf16[2560,8,256]{2,0,1:T(8,128)(2,1)}, s32[]{:T(128)}, /*index=5*/s32[]{:T(128)}, s32[]{:T(128)}, s32[]{:T(128)}) while((s32[]{:T(128)}, f32[256,8,16]{0,2,1:T(8,128)S(1)}, f32[2560,128]{1,0:T(8,128)}, bf16[2560,8,256]{2,0,1:T(8,128)(2,1)}, ...), condition=%wide.region_2.0_spmd.clone, body=%wide.region_1.0_spmd.clone.sunk | while | flops 201392128 | bytes 3670173 | solution.py:42
  154.0 1.0 constant_dynamic-slice_fusion.2
  154.9 0.1 copy.22
  155.1 2.5 fusion.32
  157.6 1.0 constant_dynamic-slice_fusion.2
  158.6 0.1 copy.22
  158.7 2.5 fusion.32
  161.3 1.0 constant_dynamic-slice_fusion.2
  162.3 0.1 copy.22
  162.4 2.5 fusion.32
  165.0 1.0 constant_dynamic-slice_fusion.2
  165.9 0.1 copy.22
  166.1 2.5 fusion.32
  168.6 1.0 constant_dynamic-slice_fusion.2
  169.6 0.1 copy.22
  169.7 2.5 fusion.32
  172.3 0.0 copy-start.1
  172.3 0.7 copy-done.1
  173.0 0.0 all-reduce.4.cloned.1.call-update
  173.0 0.0 reduce-scatter.7.cloned.1.call-start
  173.0 4.6 convert_reduce_fusion
  177.7 0.0 copy-done.3
  177.7 0.6 dynamic-slice
  178.9 57.8 %all-reduce.1 = f32[256,8]{0,1:T(8,128)S(1)} all-reduce(f32[256,8]{0,1:T(8,128)S(1)} %bitcast.41), channel_id=4, replica_groups=mesh['row'=32,'feat'=8] {'row'}, use_global_device_ids=true, to_apply=%region_5.0.clone | all-reduce | flops 2048 | bytes 16384
  236.7 0.1 dynamic-slice_add_fusion
  236.8 138.9 %all-reduce.4.cloned.1.call-done = f32[256,128]{0,1:T(8,128)} async-done(((f32[256,128]{0,1:T(8,128)}), f32[256,128]{0,1:T(8,128)}) %all-reduce.4.cloned.1.call-update) | async-done | bytes 131088
  375.6 0.9 fusion.19
  376.6 0.1 copy.13
  376.6 30.6 %all_gather.3 = bf16[256,128]{1,0:T(8,128)(2,1)S(1)} all-gather(bf16[8,128]{1,0:T(8,128)(2,1)S(1)} %copy.13), channel_id=1, replica_groups=mesh['row'=32,'feat'=8] {'row'}, dimensions={0}, use_global_device_ids=true | all-gather | bytes 67584 | tf_op jit(solution)/shard_map/all_gather | solution.py:67
  407.2 0.1 copy.14
  407.3 7.1 %fusion.14 = bf16[8,16,2560]{2,1,0:T(8,128)(2,1)S(1)} fusion(bf16[256,8,16]{0,2,1:T(8,128)(2,1)S(1)} %bitcast.40, s32[2560,8]{0,1:T(8,128)S(1)} %copy-done.2, bf16[2560]{0:T(1024)(128)(2,1)S(1)} %fusion.17), kind=kOutput, calls=%fused_computation.12 | convolution fusion | flops 178585600 | bytes 807936 | tf_op jit(solution)/shard_map/nmk,kmd->nmd/dot_general | solution.py:21
  414.5 0.4 stack.2
  414.9 67.0 %all_to_all.5 = bf16[8,2560,128]{1,2,0:T(8,128)(2,1)S(1)} all-to-all(bf16[8,2560,128]{1,2,0:T(8,128)(2,1)S(1)} %stack.2), channel_id=1, replica_groups=mesh['row'=32,'feat'=8] {'feat'}, dimensions={0} | all-to-all | bytes 10485760 | tf_op jit(solution)/shard_map/all_to_all | solution.py:49
  481.9 2.3 convolution_multiply_fusion
  484.2 0.0 reduce-scatter.7.cloned.1.call-update
  484.3 0.7 copy.15
  484.9 114.2 %reduce-scatter.7.cloned.1.call-done = f32[32,128]{1,0:T(8,128)} async-done(((f32[1024,128]{1,0:T(8,128)}), f32[32,128]{1,0:T(8,128)}) %reduce-scatter.7.cloned.1.call-update) | async-done | bytes 16400 | tf_op jit(solution)/shard_map/reduce_scatter | solution.py:74
  (2 shorter events, 0.0 us)
Async XLA Ops:
  7.2 1.1 copy-start
  7.2 8.3 %copy-start.2 = (s32[2560,8]{0,1:T(8,128)S(1)}, s32[2560,8]{0,1:T(8,128)}, u32[]{:S(2)}) copy-start(s32[2560,8]{0,1:T(8,128)} %param.8) | copy-start | bytes 245764
  7.2 146.8 %reduce-scatter.5.cloned.1.call-start = ((), (), s32[]{:S(2)}) async-start(), calls=%async_computation.3 | async-start | bytes 11796480 | tf_op jit(solution)/shard_map/reduce_scatter | solution.py:60
  14.7 360.9 %all-reduce.4.cloned.1.call-start = ((), (), s32[]{:S(2)}) async-start(), calls=%async_computation.5 | async-start | bytes 262144
  20.9 156.7 %copy-start.3 = (u32[256]{0:T(256)S(1)}, u32[256]{0:T(256)}, u32[]{:S(2)}) copy-start(u32[256]{0:T(256)} %constant.42) | copy-start | bytes 3076
  172.3 0.7 copy-start.1
  173.0 426.2 %reduce-scatter.7.cloned.1.call-start = ((), (), s32[]{:S(2)}) async-start(), calls=%async_computation.4 | async-start | bytes 540672 | tf_op jit(solution)/shard_map/reduce_scatter | solution.py:74
Sparse Core Ops, SparseCore 0:
  14.8 139.0 reduce-scatter.4
  173.1 202.5 all-reduce.3
  484.4 114.6 reduce-scatter.6
